TPU v7x, 256 devices: a whole 4x4x8 slice. The times are simulated.
256 devices in a mesh: grp: 8 (over x, core), cell: 32 (over y, z).
Axes of the slice: x: 4, y: 4, z: 8, core: 2. Of those that a mesh axis runs over, the one named last changes fastest.
Arguments:
- rhs: float32 [128, 2, 128, 16, 128], P('grp', None, 'cell'), may hold values from -8 to 8
- log_perm: float32 [128, 128, 16, 128], P('grp', 'cell'), may hold values from -1.5 to 1.5
- porosity: float32 [128, 128, 16, 128], P('grp', 'cell'), may hold values from 0.1 to 0.3
- saturation: float32 [128, 128, 16, 128], P('grp', 'cell'), may hold values from 0.2 to 0.8
- pressure: float32 [128, 128, 16, 128], P('grp', 'cell'), may hold values from -6 to 6
- obs_values: float32 [256], replicated, may hold values from -6 to 6
- obs_error: float32 [256], replicated, may hold values from 0.1 to 1
- noise: float32 [128, 256], replicated, may hold values from -6 to 6
- well_cell: int32 [128], replicated, may hold values from 0 to 262143
- obs_well: int32 [256], replicated, may hold values from 0 to 127
Outputs:
- increment: float32 [128, 2, 128, 16, 128], P('grp', None, 'cell')
- log_perm_post: float32 [128, 128, 16, 128], P('grp', 'cell')
- porosity_post: float32 [128, 128, 16, 128], P('grp', 'cell')
All inputs are finite; a program needn't handle non-finite values.
Results may differ from a plain program's by a relative error of at most 0.0003.
Values sent between devices are 32-bit elements; how exact they have to be, the bound alone decides.
No kernel may reach another device: no remote copies, remote signals or barrier semaphores. Data moves between devices by JAX's collectives and lax.ppermute only.
A program may use at most 128 MiB of HBM per device.

v0:
```python
import math
import jax
import jax.numpy as jnp
from jax import lax
from jax.sharding import Mesh
from jax.sharding import PartitionSpec as P

KRYLOV = 4
epsilon = 1e-06
time_step = 0.1
compress = 0.5
inflation = 4.0
CELL = ("cy", "cz")


def cell_sum(values, doubling=False):
    for axis in ("cz", "cy"):
        size = lax.axis_size(axis)
        if not doubling or size & size - 1:
            values = lax.psum(values, axis)
            continue
        step = 1
        while step < size:
            values = values + lax.ppermute(values, axis, [(i, i ^ step) for i in range(size)])
            step *= 2
    return values


def with_halo(block, sides, width):
    for axis, dim in sides:
        count = lax.axis_size(axis[0]) * lax.axis_size(axis[1])
        forward = [(i, i + 1) for i in range(count - 1)]
        backward = [(target, source) for source, target in forward]
        low = lax.ppermute(
            lax.slice_in_dim(block, block.shape[dim] - width, None, axis=dim), axis, forward
        )
        high = lax.ppermute(lax.slice_in_dim(block, 0, width, axis=dim), axis, backward)
        block = jnp.concatenate([low, block, high], axis=dim)
    return block


def mobility(sat_field):
    return sat_field * sat_field + 0.5 * (1.0 - sat_field) * (1.0 - sat_field)


def face_pair(perm_low, perm_high, sat_low, sat_high):
    trans = (
        2.0
        * perm_low
        * perm_high
        / (perm_low + perm_high)
        * (0.5 * (mobility(sat_low) + mobility(sat_high)))
    )
    return (trans, trans * (0.5 * (sat_low + sat_high)))


def plane_faces(perm, sat_field):
    plane_rows = perm.shape[-2]
    plane_cols = perm.shape[-1]
    keep_rows = (
        lax.broadcasted_iota(jnp.int32, (plane_rows, plane_cols), 0) < plane_rows - 1
    ).astype(jnp.float32)
    keep_cols = (
        lax.broadcasted_iota(jnp.int32, (plane_rows, plane_cols), 1) < plane_cols - 1
    ).astype(jnp.float32)
    trans_y, frac_y = face_pair(
        perm, jnp.roll(perm, -1, -2), sat_field, jnp.roll(sat_field, -1, -2)
    )
    trans_z, frac_z = face_pair(
        perm, jnp.roll(perm, -1, -1), sat_field, jnp.roll(sat_field, -1, -1)
    )
    return (trans_y * keep_rows, frac_y * keep_rows, trans_z * keep_cols, frac_z * keep_cols)


def operator(padded, second, coeffs):
    accum, trans_x, frac_x, trans_y, frac_y, trans_z, frac_z = coeffs
    first = padded[..., 1:-1, :, :]
    diff_x = padded[..., 1:, :, :] - padded[..., :-1, :, :]
    diff_y = jnp.roll(first, -1, -2) - first
    diff_z = jnp.roll(first, -1, -1) - first

    def net(coef_x, coef_y, coef_z):
        flow_x = coef_x * diff_x
        flow_y = coef_y * diff_y
        flow_z = coef_z * diff_z
        return (
            flow_x[..., :-1, :, :]
            - flow_x[..., 1:, :, :]
            + (jnp.roll(flow_y, 1, -2) - flow_y)
            + (jnp.roll(flow_z, 1, -1) - flow_z)
        )

    out_pressure = accum * (compress * first + 0.5 * second) + net(trans_x, trans_y, trans_z)
    out_water = accum * second + net(frac_x, frac_y, frac_z)
    return (out_pressure, out_water)


def least_squares(columns, beta):
    rows = [list(column) for column in columns]
    cosines = []
    sines = []
    target = [beta] + [jnp.zeros_like(beta) for column in columns]
    for jdx in range(len(rows)):
        column = rows[jdx]
        for idx in range(jdx):
            upper = cosines[idx] * column[idx] + sines[idx] * column[idx + 1]
            column[idx + 1] = -sines[idx] * column[idx] + cosines[idx] * column[idx + 1]
            column[idx] = upper
        radius = jnp.sqrt(column[jdx] * column[jdx] + column[jdx + 1] * column[jdx + 1])
        cosines.append(column[jdx] / radius)
        sines.append(column[jdx + 1] / radius)
        column[jdx] = radius
        target[jdx + 1] = -sines[jdx] * target[jdx]
        target[jdx] = cosines[jdx] * target[jdx]
    count = len(rows)
    solved = [None] * count
    for jdx in reversed(range(count)):
        partial_sum = target[jdx]
        for idx in range(jdx + 1, count):
            partial_sum = partial_sum - rows[idx][jdx] * solved[idx]
        solved[jdx] = partial_sum / rows[jdx][jdx]
    return solved


def ensemble_weights(predicted, obs_values, obs_error, noise, offset, count):
    members = predicted.shape[0]
    sigma = math.sqrt(inflation) * obs_error
    center = jnp.mean(predicted, axis=0)
    spread = (predicted - center) / (math.sqrt(members - 1.0) * sigma)
    innov = (obs_values + sigma * noise - predicted) / sigma
    own_innov = lax.dynamic_slice_in_dim(innov, offset, count, 0)
    gram = jnp.eye(members, dtype=jnp.float32) + jnp.dot(
        spread, spread.T, precision=lax.Precision.HIGHEST, preferred_element_type=jnp.float32
    )
    cross = jnp.dot(
        spread, own_innov.T, precision=lax.Precision.HIGHEST, preferred_element_type=jnp.float32
    )
    factor = jnp.linalg.cholesky(gram)
    return jax.scipy.linalg.cho_solve((factor, True), cross)


def expand(values):
    return values[:, None, None, None, None]


def inner(left, right):
    return jnp.sum(left * right, axis=(1, 2, 3, 4))


def local(
    rhs, log_perm, porosity, saturation, pressure, obs_values, obs_error, noise, well_cell, obs_well
):
    local_members, slab_x, plane_rows, plane_cols = log_perm.shape
    members = noise.shape[0]
    plane = plane_rows * plane_cols
    cells_dev = slab_x * plane
    slab_index = lax.axis_index("cy") * lax.axis_size("cz") + lax.axis_index("cz")
    slab_count = lax.axis_size("cy") * lax.axis_size("cz")
    count = slab_count
    forward = [(i, i + 1) for i in range(count - 1)]
    backward = [(target, source) for source, target in forward]
    edges = (log_perm, saturation, rhs[:, 0])
    low = lax.ppermute(jnp.stack([field[:, -1:] for field in edges], 1), CELL, forward)
    high = lax.ppermute(jnp.stack([field[:, :1] for field in edges], 1), CELL, backward)
    perm_pad = jnp.exp(jnp.concatenate([low[:, 0], log_perm, high[:, 0]], axis=1))
    sat_pad = jnp.concatenate([low[:, 1], saturation, high[:, 1]], axis=1)
    trans_x, frac_x = face_pair(perm_pad[:, :-1], perm_pad[:, 1:], sat_pad[:, :-1], sat_pad[:, 1:])
    face_pos = lax.broadcasted_iota(jnp.int32, (slab_x + 1, 1, 1), 0)
    keep_face = jnp.where(
        face_pos == 0,
        slab_index > 0,
        jnp.where(face_pos == slab_x, slab_index < slab_count - 1, True),
    ).astype(jnp.float32)
    trans_x = trans_x * keep_face
    frac_x = frac_x * keep_face
    trans_y, frac_y, trans_z, frac_z = plane_faces(perm_pad[:, 1:-1], saturation)
    coeffs = (porosity / time_step, trans_x, frac_x, trans_y, frac_y, trans_z, frac_z)

    def planes(field):
        low = lax.ppermute(field[:, -1:], CELL, forward)
        high = lax.ppermute(field[:, :1], CELL, backward)
        return (low, high)

    def apply(vector, ghosts):
        padded = jnp.concatenate([ghosts[0], vector[:, 0], ghosts[1]], axis=1)
        out_pressure, out_water = operator(padded, vector[:, 1], coeffs)
        return jnp.stack([out_pressure, out_water], 1)

    def scale_planes(ghosts, scale):
        factor = scale[:, None, None, None]
        return (ghosts[0] / factor, ghosts[1] / factor)

    rhs_planes = (low[:, 2], high[:, 2])
    image = apply(rhs, rhs_planes)
    image_planes = planes(image[:, 0])
    reduced = cell_sum(jnp.stack([inner(rhs, rhs), inner(rhs, image)], 0))
    beta = jnp.sqrt(reduced[0] + epsilon)
    basis = [rhs / expand(beta)]
    basis_planes = [scale_planes(rhs_planes, beta)]
    image = image / expand(beta)
    image_planes = scale_planes(image_planes, beta)
    projected = [reduced[1] / (beta * beta)]
    columns = []
    for jdx in range(KRYLOV):
        ortho = image
        ortho_low, ortho_high = image_planes
        for idx in range(jdx + 1):
            ortho = ortho - expand(projected[idx]) * basis[idx]
            factor = projected[idx][:, None, None, None]
            ortho_low = ortho_low - factor * basis_planes[idx][0]
            ortho_high = ortho_high - factor * basis_planes[idx][1]
        ortho_planes = (ortho_low, ortho_high)
        if jdx == KRYLOV - 1:
            height = jnp.sqrt(cell_sum(inner(ortho, ortho)) + epsilon)
            columns.append(projected + [height])
            break
        image = apply(ortho, ortho_planes)
        image_planes = planes(image[:, 0])
        parts = [inner(ortho, ortho)]
        parts += [inner(basis[idx], image) for idx in range(jdx + 1)]
        parts.append(inner(ortho, image))
        reduced = cell_sum(jnp.stack(parts, 0))
        height = jnp.sqrt(reduced[0] + epsilon)
        columns.append(projected + [height])
        basis.append(ortho / expand(height))
        basis_planes.append(scale_planes(ortho_planes, height))
        image = image / expand(height)
        image_planes = scale_planes(image_planes, height)
        projected = [reduced[1 + idx] / height for idx in range(jdx + 1)]
        projected.append(reduced[jdx + 2] / (height * height))
    solved = least_squares(columns, beta)
    increment = expand(solved[0]) * basis[0]
    for jdx in range(1, KRYLOV):
        increment = increment + expand(solved[jdx]) * basis[jdx]
    cells = jnp.take(well_cell, obs_well)
    wells = well_cell.shape[0]
    component = (jnp.arange(obs_well.shape[0], dtype=jnp.int32) >= wells).astype(jnp.int32)
    slab_row = cells // plane - slab_index * slab_x
    inside = (slab_row >= 0) & (slab_row < slab_x)
    rows = 2 * slab_x * plane_rows
    row = component * (slab_x * plane_rows) + slab_row * plane_rows + cells % plane // plane_cols
    col_z = cells % plane_cols
    state = jnp.stack([pressure + increment[:, 0], saturation + increment[:, 1]], 1)
    table = state.reshape(local_members * rows, plane_cols)
    pick_z = lax.broadcasted_iota(jnp.int32, (plane_cols, cells.shape[0]), 0) == col_z[None, :]
    by_row = jnp.dot(
        table,
        pick_z.astype(jnp.float32),
        precision=lax.Precision.HIGHEST,
        preferred_element_type=jnp.float32,
    )
    pick_row = (
        lax.broadcasted_iota(jnp.int32, (rows, cells.shape[0]), 0) == row[None, :]
    ) & inside[None, :]
    picked = jnp.sum(
        by_row.reshape(local_members, rows, cells.shape[0]) * pick_row.astype(jnp.float32)[None],
        axis=1,
    )
    slab_pred = cell_sum(picked, doubling=True)
    predicted = lax.all_gather(slab_pred, "grp", axis=0, tiled=True)
    params = jnp.stack([log_perm, porosity], 1).reshape(local_members, 2 * cells_dev)
    offset = lax.axis_index("grp") * local_members
    own_columns = ensemble_weights(predicted, obs_values, obs_error, noise, offset, local_members)
    scale_factor = 1.0 / math.sqrt(members - 1.0)
    scaled = params * scale_factor
    update = jnp.dot(
        own_columns.T,
        lax.all_gather(scaled, "grp", axis=0, tiled=True),
        precision=lax.Precision.HIGHEST,
        preferred_element_type=jnp.float32,
    )
    posterior = params + update
    posterior = posterior.reshape(local_members, 2, slab_x, plane_rows, plane_cols)
    return (increment, posterior[:, 0], posterior[:, 1])


def split_mesh(mesh):
    devices = mesh.devices
    groups, slabs = devices.shape
    along_z = len({device.coords[2] for device in devices[0]})
    return Mesh(devices.reshape(groups, slabs // along_z, along_z), ("grp", "cy", "cz"))


def solution(mesh):
    mesh = split_mesh(mesh)
    in_specs = (
        P("grp", None, CELL, None, None),
        P("grp", CELL, None, None),
        P("grp", CELL, None, None),
        P("grp", CELL, None, None),
        P("grp", CELL, None, None),
        P(),
        P(),
        P(),
        P(),
        P(),
    )
    out_specs = (
        P("grp", None, CELL, None, None),
        P("grp", CELL, None, None),
        P("grp", CELL, None, None),
    )
    return jax.shard_map(local, mesh=mesh, in_specs=in_specs, out_specs=out_specs, check_vma=False)
```

profile of v0, /device:TPU:1, one launch (start us, length us, event | category | flops | bytes accessed | tf_op | source)
XLA Modules:
  0.0 307.5 jit_solution(6333934453051698767)
XLA Ops:
  7.3 1.2 slice_bitcast_fusion.11
  8.5 1.0 slice_bitcast_fusion.21
  9.5 1.0 slice_bitcast_fusion.17
  10.5 0.8 pad_maximum_fusion.13
  11.3 1.3 collective-permute-start.1
  12.6 0.8 pad_maximum_fusion.12
  13.3 5.0 %collective-permute-start = (f32[16,3,1,16,128]{4,3,0,2,1:T(8,128)}, f32[16,3,1,16,128]{4,3,0,2,1:T(8,128)S(1)}, u32[]{:S(2)}, u32[]{:S(2)}) collective-permute-start(f32[16,3,1,16,128]{4,3,0,2,1:T(8,128)} %pad_maximum_fusion.12), channel_id=1, source_target_pairs={{0,1},{1,2},{2,3},{3,4},{4,5},{5,6},{6,7},{7,8},{8,9},{9,10},{10,1... | collective-permute-start | bytes 1179656 | tf_op jit(solution)/shard_map/ppermute | solution.py:163
  18.3 1.3 pad_maximum_fusion.4
  19.8 1.1 copy-done.23
  20.8 1.6 bitcast_multiply_fusion
  22.6 1.9 gather_fusion
  25.1 0.7 fusion.60
  27.1 1.2 fusion.56
  28.4 1.3 fusion.55
  29.7 1.0 multiply_multiply_fusion.11
  31.0 1.6 fusion.94
  34.1 19.3 %psum.70 = f32[2,16]{1,0:T(2,128)S(1)} all-reduce(f32[2,16]{1,0:T(2,128)S(1)} %pad_maximum_fusion.16), channel_id=1, replica_groups=mesh['grp'=8,'cy'=4,'cz'=8] {'cz'}, use_global_device_ids=true, to_apply=%region_2.3 | all-reduce | flops 32 | bytes 256 | tf_op jit(solution)/shard_map/psum | solution.py:20
  53.5 10.3 %psum.71 = f32[2,16]{1,0:T(2,128)S(1)} all-reduce(f32[2,16]{1,0:T(2,128)S(1)} %psum.70), channel_id=1, replica_groups=mesh['grp'=8,'cy'=4,'cz'=8] {'cy'}, use_global_device_ids=true, to_apply=%region_3.4 | all-reduce | flops 32 | bytes 256 | tf_op jit(solution)/shard_map/psum | solution.py:20
  64.4 1.4 collective-permute-start.2
  65.8 4.0 %collective-permute-start.3 = (f32[16,1,16,128]{3,2,1,0:T(8,128)S(1)}, f32[16,1,16,128]{3,2,1,0:T(8,128)S(1)}, u32[]{:S(2)}, u32[]{:S(2)}) collective-permute-start(f32[16,1,16,128]{3,2,1,0:T(8,128)S(1)} %get-tuple-element.72), channel_id=1, source_target_pairs={{0,1},{1,2},{2,3},{3,4},{4,5},{5,6},{6,7},{7,8},{8,9},{9,10},{10,1... | collective-permute-start | bytes 393224 | tf_op jit(solution)/shard_map/ppermute | solution.py:180
  69.8 2.0 multiply_multiply_fusion.10
  71.8 1.2 broadcast_divide_fusion
  73.5 1.1 multiply_subtract_fusion.8
  76.6 14.2 %psum.72 = f32[3,16]{1,0:T(4,128)S(1)} all-reduce(f32[3,16]{1,0:T(4,128)S(1)} %pad_maximum_fusion.14), channel_id=1, replica_groups=mesh['grp'=8,'cy'=4,'cz'=8] {'cz'}, use_global_device_ids=true, to_apply=%region_7.8 | all-reduce | flops 48 | bytes 384 | tf_op jit(solution)/shard_map/psum | solution.py:20
  90.9 6.0 %psum.73 = f32[3,16]{1,0:T(4,128)S(1)} all-reduce(f32[3,16]{1,0:T(4,128)S(1)} %psum.72), channel_id=1, replica_groups=mesh['grp'=8,'cy'=4,'cz'=8] {'cy'}, use_global_device_ids=true, to_apply=%region_8.9 | all-reduce | flops 48 | bytes 384 | tf_op jit(solution)/shard_map/psum | solution.py:20
  97.4 2.6 multiply_subtract_fusion.1
  100.4 1.3 collective-permute-start.4
  101.7 4.2 %collective-permute-start.5 = (f32[16,1,16,128]{3,2,1,0:T(8,128)S(1)}, f32[16,1,16,128]{3,2,1,0:T(8,128)S(1)}, u32[]{:S(2)}, u32[]{:S(2)}) collective-permute-start(f32[16,1,16,128]{3,2,1,0:T(8,128)S(1)} %get-tuple-element.70), channel_id=1, source_target_pairs={{0,1},{1,2},{2,3},{3,4},{4,5},{5,6},{6,7},{7,8},{8,9},{9,10},{10,1... | collective-permute-start | bytes 393224 | tf_op jit(solution)/shard_map/ppermute | solution.py:180
  105.9 2.0 multiply_multiply_fusion.9
  108.4 1.3 multiply_subtract_fusion.6
  111.4 0.7 multiply_reduce_fusion.10
  112.2 14.7 %psum.74 = f32[4,16]{1,0:T(4,128)} all-reduce(f32[4,16]{1,0:T(4,128)S(1)} %pad_maximum_fusion.15), channel_id=1, replica_groups=mesh['grp'=8,'cy'=4,'cz'=8] {'cz'}, use_global_device_ids=true, to_apply=%region_13.14 | all-reduce | flops 64 | bytes 512 | tf_op jit(solution)/shard_map/psum | solution.py:20
  126.9 7.4 %psum.75 = f32[4,16]{1,0:T(4,128)} all-reduce(f32[4,16]{1,0:T(4,128)} %psum.74), channel_id=1, replica_groups=mesh['grp'=8,'cy'=4,'cz'=8] {'cy'}, use_global_device_ids=true, to_apply=%region_14.15 | all-reduce | flops 64 | bytes 512 | tf_op jit(solution)/shard_map/psum | solution.py:20
  134.4 0.8 sqrt_bitcast_fusion.1
  135.2 0.8 bitcast_divide_fusion.4
  136.1 2.4 copy_subtract_fusion
  138.9 1.4 collective-permute-start.6
  140.3 4.0 %collective-permute-start.7 = (f32[16,1,16,128]{3,2,1,0:T(8,128)S(1)}, f32[16,1,16,128]{3,2,1,0:T(8,128)S(1)}, u32[]{:S(2)}, u32[]{:S(2)}) collective-permute-start(f32[16,1,16,128]{3,2,1,0:T(8,128)S(1)} %get-tuple-element.68), channel_id=1, source_target_pairs={{0,1},{1,2},{2,3},{3,4},{4,5},{5,6},{6,7},{7,8},{8,9},{9,10},{10,1... | collective-permute-start | bytes 393224 | tf_op jit(solution)/shard_map/ppermute | solution.py:180
  144.4 1.2 multiply_multiply_fusion.8
  146.2 1.2 multiply_subtract_fusion.4
  148.7 0.9 multiply_reduce_fusion.2
  149.6 14.1 %psum.76 = f32[5,16]{1,0:T(8,128)S(1)} all-reduce(f32[5,16]{1,0:T(8,128)S(1)} %stack.169), channel_id=1, replica_groups=mesh['grp'=8,'cy'=4,'cz'=8] {'cz'}, use_global_device_ids=true, to_apply=%region_20.21 | all-reduce | flops 80 | bytes 640 | tf_op jit(solution)/shard_map/psum | solution.py:20
  163.7 7.9 %psum.77 = f32[5,16]{1,0:T(8,128)S(1)} all-reduce(f32[5,16]{1,0:T(8,128)S(1)} %psum.76), channel_id=1, replica_groups=mesh['grp'=8,'cy'=4,'cz'=8] {'cy'}, use_global_device_ids=true, to_apply=%region_21.22 | all-reduce | flops 80 | bytes 640 | tf_op jit(solution)/shard_map/psum | solution.py:20
  171.7 2.3 multiply_reduce_fusion.1
  174.0 12.3 %psum.78 = f32[16]{0:T(128)S(1)} all-reduce(f32[16]{0:T(128)S(1)} %multiply_reduce_fusion.1), channel_id=1, replica_groups=mesh['grp'=8,'cy'=4,'cz'=8] {'cz'}, use_global_device_ids=true, to_apply=%region_23.24 | all-reduce | flops 16 | bytes 128 | tf_op jit(solution)/shard_map/psum | solution.py:20
  186.3 6.1 %psum.79 = f32[16]{0:T(128)S(1)} all-reduce(f32[16]{0:T(128)S(1)} %psum.78), channel_id=1, replica_groups=mesh['grp'=8,'cy'=4,'cz'=8] {'cy'}, use_global_device_ids=true, to_apply=%region_24.25 | all-reduce | flops 16 | bytes 128 | tf_op jit(solution)/shard_map/psum | solution.py:20
  192.5 2.1 multiply_add_fusion
  194.6 1.6 fusion.19
  196.4 1.0 multiply_reduce_fusion
  197.7 2.5 collective-permute-done.8
  200.1 3.5 %collective-permute-done.9 = f32[16,256]{1,0:T(8,128)S(1)} collective-permute-done((f32[16,256]{1,0:T(8,128)S(1)}, f32[16,256]{1,0:T(8,128)S(1)}, u32[]{:S(2)}, u32[]{:S(2)}) %collective-permute-start.9) | collective-permute-done | bytes 16416 | tf_op jit(solution)/shard_map/ppermute | solution.py:24
  203.7 2.3 collective-permute-start.10
  205.9 4.4 %collective-permute-done.10 = f32[16,256]{1,0:T(8,128)S(1)} collective-permute-done((f32[16,256]{1,0:T(8,128)S(1)}, f32[16,256]{1,0:T(8,128)S(1)}, u32[]{:S(2)}, u32[]{:S(2)}) %collective-permute-start.10) | collective-permute-done | bytes 16416 | tf_op jit(solution)/shard_map/ppermute | solution.py:24
  210.3 1.4 collective-permute-start.11
  211.7 1.2 collective-permute-done.11
  212.9 0.9 collective-permute-start.12
  213.8 3.2 %collective-permute-done.12 = f32[16,256]{1,0:T(8,128)S(1)} collective-permute-done((f32[16,256]{1,0:T(8,128)S(1)}, f32[16,256]{1,0:T(8,128)S(1)}, u32[]{:S(2)}, u32[]{:S(2)}) %collective-permute-start.12) | collective-permute-done | bytes 16416 | tf_op jit(solution)/shard_map/ppermute | solution.py:24
  217.0 50.4 %all_gather.6 = f32[128,256]{1,0:T(8,128)S(1)} all-gather(f32[16,256]{1,0:T(8,128)S(1)} %add.480), channel_id=1, replica_groups=mesh['grp'=8,'cy'=4,'cz'=8] {'grp'}, dimensions={0}, use_global_device_ids=true | all-gather | bytes 147456 | tf_op jit(solution)/shard_map/all_gather | solution.py:260
  267.9 11.7 %cholesky.17 = f32[128,128]{1,0:T(8,128)S(1)} custom-call(f32[128,128]{1,0:T(8,128)S(1)} %fusion.71), custom_call_target="Cholesky" | custom-call | tf_op jit(solution)/shard_map/jit(cholesky)/cholesky | solution.py:138
  280.3 0.7 fusion.65
  280.9 9.8 %custom-call.10 = f32[1,128,128]{1,2,0:T(8,128)S(1)} custom-call(f32[1,128,128]{2,1,0:T(8,128)S(1)} %fusion.65), custom_call_target="InvertDiagBlocksLowerTriangular" | custom-call | tf_op jit(solution)/shard_map/jit(_cho_solve)/triangular_solve | solution.py:139
  290.8 1.0 fusion.73
  292.3 7.1 %fusion = f32[2,8,128,128]{3,1,2,0:T(8,128)S(1)} fusion(f32[128,16]{1,0:T(8,128)S(1)} %fusion.66, f32[128,16384]{1,0:T(8,128)} %all-gather.2.cloned.1.call-done, f32[2,8,128,128]{3,2,1,0:T(8,128)S(1)} %bitcast.504), kind=kOutput, calls=%fused_computation.3 | convolution fusion | flops 402915328 | bytes 10493952 | tf_op jit(solution)/shard_map/dot_general | solution.py:266
  299.6 1.1 slice_bitcast_fusion
  (225 shorter events, 14.7 us)
Async XLA Ops:
  7.2 15.4 %copy-start = (s32[128]{0:T(128)S(1)}, s32[128]{0:T(128)}, u32[]{:S(2)}) copy-start(s32[128]{0:T(128)} %param.18) | copy-start | bytes 1540
  7.2 19.2 %copy-start.2 = (f32[16,2,4,16,128]{4,3,2,1,0:T(8,128)S(1)}, f32[16,2,4,16,128]{4,3,2,1,0:T(8,128)}, u32[]{:S(2)}) copy-start(f32[16,2,4,16,128]{4,3,2,1,0:T(8,128)} %param.10) | copy-start | bytes 3145732
  7.2 18.9 %copy-start.3 = (f32[16,4,16,128]{3,2,1,0:T(8,128)S(1)}, f32[16,4,16,128]{3,2,1,0:T(8,128)}, u32[]{:S(2)}) copy-start(f32[16,4,16,128]{3,2,1,0:T(8,128)} %param.13) | copy-start | bytes 1572868
  7.2 15.3 %copy-start.53 = (s32[256]{0:T(256)S(1)}, s32[256]{0:T(256)}, u32[]{:S(2)}) copy-start(s32[256]{0:T(256)} %param.19) | copy-start | bytes 3076
  7.2 285.1 %all-gather.2.cloned.1.call-start = ((), (), s32[]{:S(2)}) async-start(), calls=%async_computation | async-start | bytes 9437184 | tf_op jit(solution)/shard_map/all_gather | solution.py:268
  10.5 16.2 %copy-start.27 = (f32[16,4,16,128]{3,2,1,0:T(8,128)S(1)}, f32[16,4,16,128]{3,2,1,0:T(8,128)}, u32[]{:S(2)}) copy-start(f32[16,4,16,128]{3,2,1,0:T(8,128)} %param.11) | copy-start | bytes 1572868
  11.3 15.3 %collective-permute-start.1 = (f32[16,3,1,16,128]{4,3,0,2,1:T(8,128)}, f32[16,3,1,16,128]{4,3,0,2,1:T(8,128)S(1)}, u32[]{:S(2)}, u32[]{:S(2)}) collective-permute-start(f32[16,3,1,16,128]{4,3,0,2,1:T(8,128)} %pad_maximum_fusion.13), channel_id=1, source_target_pairs={{1,0},{2,1},{3,2},{4,3},{5,4},{6,5},{7,6},{8,7},{9,8},{10,9},{11,1... | collective-permute-start | bytes 1179656 | tf_op jit(solution)/shard_map/ppermute | solution.py:164
  13.3 13.3 %collective-permute-start = (f32[16,3,1,16,128]{4,3,0,2,1:T(8,128)}, f32[16,3,1,16,128]{4,3,0,2,1:T(8,128)S(1)}, u32[]{:S(2)}, u32[]{:S(2)}) collective-permute-start(f32[16,3,1,16,128]{4,3,0,2,1:T(8,128)} %pad_maximum_fusion.12), channel_id=1, source_target_pairs={{0,1},{1,2},{2,3},{3,4},{4,5},{5,6},{6,7},{7,8},{8,9},{9,10},{10,1... | collective-permute-start | bytes 1179656 | tf_op jit(solution)/shard_map/ppermute | solution.py:163
  25.8 80.1 %copy-start.43 = (f32[128]{0:T(128)}, f32[128]{0:T(128)S(1)}, u32[]{:S(2)}) copy-start(f32[128]{0:T(128)S(1)} %compare_convert_fusion) | copy-start | bytes 1540
  25.8 80.1 %copy-start.44 = (f32[16]{0:T(128)}, f32[16]{0:T(128)S(1)}, u32[]{:S(2)}) copy-start(f32[16]{0:T(128)S(1)} %compare_convert_fusion.1) | copy-start | bytes 196
  26.6 4.1 %copy-start.37 = (f32[16,3,1,16,128]{4,3,0,2,1:T(8,128)}, f32[16,3,1,16,128]{4,3,0,2,1:T(8,128)S(1)}, u32[]{:S(2)}) copy-start(f32[16,3,1,16,128]{4,3,0,2,1:T(8,128)S(1)} %collective-permute-done.1) | copy-start | bytes 1179652
  26.6 4.1 %copy-start.38 = (f32[16,3,1,16,128]{4,3,0,2,1:T(8,128)}, f32[16,3,1,16,128]{4,3,0,2,1:T(8,128)S(1)}, u32[]{:S(2)}) copy-start(f32[16,3,1,16,128]{4,3,0,2,1:T(8,128)S(1)} %collective-permute-done) | copy-start | bytes 1179652
  29.7 3.1 %copy-start.8 = (f32[16,4,16,128]{3,2,1,0:T(8,128)S(1)}, f32[16,4,16,128]{3,2,1,0:T(8,128)}, u32[]{:S(2)}) copy-start(f32[16,4,16,128]{3,2,1,0:T(8,128)} %param.12) | copy-start | bytes 1572868
  30.7 3.2 %copy-start.13 = (f32[16,4,16,128]{3,2,1,0:T(8,128)}, f32[16,4,16,128]{3,2,1,0:T(8,128)S(1)}, u32[]{:S(2)}) copy-start(f32[16,4,16,128]{3,2,1,0:T(8,128)S(1)} %get-tuple-element.24) | copy-start | bytes 1572868
  30.7 3.2 %copy-start.15 = (f32[16,4,16,128]{3,2,1,0:T(8,128)}, f32[16,4,16,128]{3,2,1,0:T(8,128)S(1)}, u32[]{:S(2)}) copy-start(f32[16,4,16,128]{3,2,1,0:T(8,128)S(1)} %get-tuple-element.36) | copy-start | bytes 1572868
  33.9 41.9 %copy-start.5 = (f32[16,1,4,16,128]{4,3,2,0,1:T(8,128)}, f32[16,1,4,16,128]{4,3,2,0,1:T(8,128)S(1)}, u32[]{:S(2)}) copy-start(f32[16,1,4,16,128]{4,3,2,0,1:T(8,128)S(1)} %fusion.45) | copy-start | bytes 1572868
  63.7 33.1 %copy-start.47 = (f32[2,16]{1,0:T(2,128)}, f32[2,16]{1,0:T(2,128)S(1)}, u32[]{:S(2)}) copy-start(f32[2,16]{1,0:T(2,128)S(1)} %psum.71) | copy-start | bytes 388
  63.8 10.8 %copy-start.17 = (f32[16,5,16,128]{3,2,1,0:T(8,128)S(1)}, f32[16,5,16,128]{3,2,1,0:T(8,128)}, u32[]{:S(2)}) copy-start(f32[16,5,16,128]{3,2,1,0:T(8,128)} %get-tuple-element.28) | copy-start | bytes 1966084
  63.8 10.8 %copy-start.20 = (f32[16,5,16,128]{3,2,1,0:T(8,128)S(1)}, f32[16,5,16,128]{3,2,1,0:T(8,128)}, u32[]{:S(2)}) copy-start(f32[16,5,16,128]{3,2,1,0:T(8,128)} %get-tuple-element.34) | copy-start | bytes 1966084
  64.0 11.3 %copy-start.12 = (f32[16,2,4,16,128]{4,3,2,0,1:T(8,128)}, f32[16,2,4,16,128]{4,3,2,0,1:T(8,128)S(1)}, u32[]{:S(2)}) copy-start(f32[16,2,4,16,128]{4,3,2,0,1:T(8,128)S(1)} %multiply_subtract_fusion.2) | copy-start | bytes 3145732
  64.4 9.1 %collective-permute-start.2 = (f32[16,1,16,128]{3,2,1,0:T(8,128)S(1)}, f32[16,1,16,128]{3,2,1,0:T(8,128)S(1)}, u32[]{:S(2)}, u32[]{:S(2)}) collective-permute-start(f32[16,1,16,128]{3,2,1,0:T(8,128)S(1)} %get-tuple-element.71), channel_id=1, source_target_pairs={{1,0},{2,1},{3,2},{4,3},{5,4},{6,5},{7,6},{8,7},{9,8},{10,9},{11,1... | collective-permute-start | bytes 393224 | tf_op jit(solution)/shard_map/ppermute | solution.py:181
  65.8 7.7 %collective-permute-start.3 = (f32[16,1,16,128]{3,2,1,0:T(8,128)S(1)}, f32[16,1,16,128]{3,2,1,0:T(8,128)S(1)}, u32[]{:S(2)}, u32[]{:S(2)}) collective-permute-start(f32[16,1,16,128]{3,2,1,0:T(8,128)S(1)} %get-tuple-element.72), channel_id=1, source_target_pairs={{0,1},{1,2},{2,3},{3,4},{4,5},{5,6},{6,7},{7,8},{8,9},{9,10},{10,1... | collective-permute-start | bytes 393224 | tf_op jit(solution)/shard_map/ppermute | solution.py:180
  96.9 11.5 %copy-start.45 = (f32[3,16]{1,0:T(4,128)}, f32[3,16]{1,0:T(4,128)S(1)}, u32[]{:S(2)}) copy-start(f32[3,16]{1,0:T(4,128)S(1)} %psum.73) | copy-start | bytes 580
  96.9 3.5 %copy-start.29 = (f32[16,4,16,128]{3,2,1,0:T(8,128)S(1)}, f32[16,4,16,128]{3,2,1,0:T(8,128)}, u32[]{:S(2)}) copy-start(f32[16,4,16,128]{3,2,1,0:T(8,128)} %copy-done.28) | copy-start | bytes 1572868
  97.4 11.0 %copy-start.51 = (f32[16]{0:T(128)}, f32[16]{0:T(128)S(1)}, u32[]{:S(2)}) copy-start(f32[16]{0:T(128)S(1)} %get-tuple-element.98) | copy-start | bytes 196
  97.4 12.3 %copy-start.18 = (f32[16,5,16,128]{3,2,1,0:T(8,128)S(1)}, f32[16,5,16,128]{3,2,1,0:T(8,128)}, u32[]{:S(2)}) copy-start(f32[16,5,16,128]{3,2,1,0:T(8,128)} %get-tuple-element.28) | copy-start | bytes 1966084
  97.4 12.3 %copy-start.21 = (f32[16,5,16,128]{3,2,1,0:T(8,128)S(1)}, f32[16,5,16,128]{3,2,1,0:T(8,128)}, u32[]{:S(2)}) copy-start(f32[16,5,16,128]{3,2,1,0:T(8,128)} %get-tuple-element.34) | copy-start | bytes 1966084
  100.0 10.3 %copy-start.9 = (f32[16,4,16,128]{3,2,1,0:T(8,128)S(1)}, f32[16,4,16,128]{3,2,1,0:T(8,128)}, u32[]{:S(2)}) copy-start(f32[16,4,16,128]{3,2,1,0:T(8,128)} %param.12) | copy-start | bytes 1572868
  100.4 8.0 %collective-permute-start.4 = (f32[16,1,16,128]{3,2,1,0:T(8,128)S(1)}, f32[16,1,16,128]{3,2,1,0:T(8,128)S(1)}, u32[]{:S(2)}, u32[]{:S(2)}) collective-permute-start(f32[16,1,16,128]{3,2,1,0:T(8,128)S(1)} %get-tuple-element.69), channel_id=1, source_target_pairs={{1,0},{2,1},{3,2},{4,3},{5,4},{6,5},{7,6},{8,7},{9,8},{10,9},{11,1... | collective-permute-start | bytes 393224 | tf_op jit(solution)/shard_map/ppermute | solution.py:181
  101.7 6.7 %collective-permute-start.5 = (f32[16,1,16,128]{3,2,1,0:T(8,128)S(1)}, f32[16,1,16,128]{3,2,1,0:T(8,128)S(1)}, u32[]{:S(2)}, u32[]{:S(2)}) collective-permute-start(f32[16,1,16,128]{3,2,1,0:T(8,128)S(1)} %get-tuple-element.70), channel_id=1, source_target_pairs={{0,1},{1,2},{2,3},{3,4},{4,5},{5,6},{6,7},{7,8},{8,9},{9,10},{10,1... | collective-permute-start | bytes 393224 | tf_op jit(solution)/shard_map/ppermute | solution.py:180
  108.1 3.3 %copy-start.6 = (f32[16,1,4,16,128]{4,3,2,0,1:T(8,128)S(1)}, f32[16,1,4,16,128]{4,3,2,0,1:T(8,128)}, u32[]{:S(2)}) copy-start(f32[16,1,4,16,128]{4,3,2,0,1:T(8,128)} %copy-done.5) | copy-start | bytes 1572868
  108.1 3.3 %copy-start.11 = (f32[16,2,4,16,128]{4,3,2,1,0:T(8,128)S(1)}, f32[16,2,4,16,128]{4,3,2,1,0:T(8,128)}, u32[]{:S(2)}) copy-start(f32[16,2,4,16,128]{4,3,2,1,0:T(8,128)} %broadcast_divide_fusion) | copy-start | bytes 3145732
  134.4 4.5 %copy-start.31 = (f32[16,4,16,128]{3,2,1,0:T(8,128)S(1)}, f32[16,4,16,128]{3,2,1,0:T(8,128)}, u32[]{:S(2)}) copy-start(f32[16,4,16,128]{3,2,1,0:T(8,128)} %copy-done.30) | copy-start | bytes 1572868
  134.4 9.9 %copy-start.14 = (f32[16,4,16,128]{3,2,1,0:T(8,128)S(1)}, f32[16,4,16,128]{3,2,1,0:T(8,128)}, u32[]{:S(2)}) copy-start(f32[16,4,16,128]{3,2,1,0:T(8,128)} %copy-done.13) | copy-start | bytes 1572868
  134.4 10.0 %copy-start.16 = (f32[16,4,16,128]{3,2,1,0:T(8,128)S(1)}, f32[16,4,16,128]{3,2,1,0:T(8,128)}, u32[]{:S(2)}) copy-start(f32[16,4,16,128]{3,2,1,0:T(8,128)} %copy-done.15) | copy-start | bytes 1572868
  134.4 10.0 %copy-start.25 = (f32[16,4,16,128]{3,2,1,0:T(8,128)S(1)}, f32[16,4,16,128]{3,2,1,0:T(8,128)}, u32[]{:S(2)}) copy-start(f32[16,4,16,128]{3,2,1,0:T(8,128)} %get-tuple-element.30) | copy-start | bytes 1572868
  134.4 10.0 %copy-start.26 = (f32[16,4,16,128]{3,2,1,0:T(8,128)S(1)}, f32[16,4,16,128]{3,2,1,0:T(8,128)}, u32[]{:S(2)}) copy-start(f32[16,4,16,128]{3,2,1,0:T(8,128)} %get-tuple-element.50) | copy-start | bytes 1572868
  136.0 10.2 %copy-start.49 = (f32[16]{0:T(128)}, f32[16]{0:T(128)S(1)}, u32[]{:S(2)}) copy-start(f32[16]{0:T(128)S(1)} %get-tuple-element.91) | copy-start | bytes 196
  136.0 10.2 %copy-start.40 = (f32[16,1,16,128]{3,2,1,0:T(8,128)S(1)}, f32[16,1,16,128]{3,2,1,0:T(8,128)}, u32[]{:S(2)}) copy-start(f32[16,1,16,128]{3,2,1,0:T(8,128)} %copy-done.39) | copy-start | bytes 393220
  136.0 11.4 %copy-start.19 = (f32[16,5,16,128]{3,2,1,0:T(8,128)S(1)}, f32[16,5,16,128]{3,2,1,0:T(8,128)}, u32[]{:S(2)}) copy-start(f32[16,5,16,128]{3,2,1,0:T(8,128)} %get-tuple-element.28) | copy-start | bytes 1966084
  136.0 11.4 %copy-start.22 = (f32[16,5,16,128]{3,2,1,0:T(8,128)S(1)}, f32[16,5,16,128]{3,2,1,0:T(8,128)}, u32[]{:S(2)}) copy-start(f32[16,5,16,128]{3,2,1,0:T(8,128)} %get-tuple-element.34) | copy-start | bytes 1966084
  138.5 10.2 %copy-start.4 = (f32[16,2,4,16,128]{4,3,2,1,0:T(8,128)}, f32[16,2,4,16,128]{4,3,2,1,0:T(8,128)S(1)}, u32[]{:S(2)}) copy-start(f32[16,2,4,16,128]{4,3,2,1,0:T(8,128)S(1)} %copy_subtract_fusion) | copy-start | bytes 3145732
  138.5 9.1 %copy-start.10 = (f32[16,4,16,128]{3,2,1,0:T(8,128)S(1)}, f32[16,4,16,128]{3,2,1,0:T(8,128)}, u32[]{:S(2)}) copy-start(f32[16,4,16,128]{3,2,1,0:T(8,128)} %param.12) | copy-start | bytes 1572868
  138.9 7.2 %collective-permute-start.6 = (f32[16,1,16,128]{3,2,1,0:T(8,128)S(1)}, f32[16,1,16,128]{3,2,1,0:T(8,128)S(1)}, u32[]{:S(2)}, u32[]{:S(2)}) collective-permute-start(f32[16,1,16,128]{3,2,1,0:T(8,128)S(1)} %get-tuple-element.67), channel_id=1, source_target_pairs={{1,0},{2,1},{3,2},{4,3},{5,4},{6,5},{7,6},{8,7},{9,8},{10,9},{11,1... | collective-permute-start | bytes 393224 | tf_op jit(solution)/shard_map/ppermute | solution.py:181
  140.3 5.9 %collective-permute-start.7 = (f32[16,1,16,128]{3,2,1,0:T(8,128)S(1)}, f32[16,1,16,128]{3,2,1,0:T(8,128)S(1)}, u32[]{:S(2)}, u32[]{:S(2)}) collective-permute-start(f32[16,1,16,128]{3,2,1,0:T(8,128)S(1)} %get-tuple-element.68), channel_id=1, source_target_pairs={{0,1},{1,2},{2,3},{3,4},{4,5},{5,6},{6,7},{7,8},{8,9},{9,10},{10,1... | collective-permute-start | bytes 393224 | tf_op jit(solution)/shard_map/ppermute | solution.py:180
  145.8 2.9 copy-start.7
  148.2 44.2 %copy-start.42 = (f32[4,16]{1,0:T(4,128)S(1)}, f32[4,16]{1,0:T(4,128)}, u32[]{:S(2)}) copy-start(f32[4,16]{1,0:T(4,128)} %psum.75) | copy-start | bytes 772
  148.2 44.2 %copy-start.46 = (f32[3,16]{1,0:T(4,128)S(1)}, f32[3,16]{1,0:T(4,128)}, u32[]{:S(2)}) copy-start(f32[3,16]{1,0:T(4,128)} %copy-done.45) | copy-start | bytes 580
  148.2 44.2 %copy-start.48 = (f32[2,16]{1,0:T(2,128)S(1)}, f32[2,16]{1,0:T(2,128)}, u32[]{:S(2)}) copy-start(f32[2,16]{1,0:T(2,128)} %copy-done.47) | copy-start | bytes 388
  148.2 44.2 %copy-start.50 = (f32[16]{0:T(128)S(1)}, f32[16]{0:T(128)}, u32[]{:S(2)}) copy-start(f32[16]{0:T(128)} %copy-done.49) | copy-start | bytes 196
  148.2 44.2 %copy-start.52 = (f32[16]{0:T(128)S(1)}, f32[16]{0:T(128)}, u32[]{:S(2)}) copy-start(f32[16]{0:T(128)} %copy-done.51) | copy-start | bytes 196
  148.2 44.2 %copy-start.55 = (f32[16]{0:T(128)S(1)}, f32[16]{0:T(128)}, u32[]{:S(2)}) copy-start(f32[16]{0:T(128)} %get-tuple-element.97) | copy-start | bytes 196
  173.9 22.5 %copy-start.41 = (f32[128,256]{1,0:T(8,128)S(1)}, f32[128,256]{1,0:T(8,128)}, u32[]{:S(2)}) copy-start(f32[128,256]{1,0:T(8,128)} %fusion.60) | copy-start | bytes 393220
  174.0 22.5 %copy-start.54 = (s32[256]{0:T(256)S(1)}, s32[256]{0:T(256)}, u32[]{:S(2)}) copy-start(s32[256]{0:T(256)} %get-tuple-element.15) | copy-start | bytes 3076
  174.0 39.9 %copy-start.56 = (f32[256]{0:T(256)S(1)}, f32[256]{0:T(256)}, u32[]{:S(2)}) copy-start(f32[256]{0:T(256)} %param.16) | copy-start | bytes 3076
  174.0 116.8 %copy-start.57 = (f32[256]{0:T(256)S(1)}, f32[256]{0:T(256)}, u32[]{:S(2)}) copy-start(f32[256]{0:T(256)} %param.15) | copy-start | bytes 3076
  194.6 1.6 copy-start.36
  194.6 97.7 %copy-start.24 = (f32[16,2,4,16,128]{4,3,2,1,0:T(8,128)S(1)}, f32[16,2,4,16,128]{4,3,2,1,0:T(8,128)}, u32[]{:S(2)}) copy-start(f32[16,2,4,16,128]{4,3,2,1,0:T(8,128)} %copy-done.23) | copy-start | bytes 3145732
  197.5 2.7 collective-permute-start.8
  200.1 3.5 %collective-permute-start.9 = (f32[16,256]{1,0:T(8,128)S(1)}, f32[16,256]{1,0:T(8,128)S(1)}, u32[]{:S(2)}, u32[]{:S(2)}) collective-permute-start(f32[16,256]{1,0:T(8,128)S(1)} %add.476), channel_id=1, source_target_pairs={{0,2},{1,3},{2,0},{3,1},{4,6},{5,7},{6,4},{7,5},{8,10},{9,11},{10,... | collective-permute-start | bytes 49160 | tf_op jit(solution)/shard_map/ppermute | solution.py:24
  203.7 6.7 %collective-permute-start.10 = (f32[16,256]{1,0:T(8,128)S(1)}, f32[16,256]{1,0:T(8,128)S(1)}, u32[]{:S(2)}, u32[]{:S(2)}) collective-permute-start(f32[16,256]{1,0:T(8,128)S(1)} %add.477), channel_id=1, source_target_pairs={{0,4},{1,5},{2,6},{3,7},{4,0},{5,1},{6,2},{7,3},{8,12},{9,13},{10,... | collective-permute-start | bytes 49160 | tf_op jit(solution)/shard_map/ppermute | solution.py:24
  210.3 2.6 collective-permute-start.11
  212.9 4.1 %collective-permute-start.12 = (f32[16,256]{1,0:T(8,128)S(1)}, f32[16,256]{1,0:T(8,128)S(1)}, u32[]{:S(2)}, u32[]{:S(2)}) collective-permute-start(f32[16,256]{1,0:T(8,128)S(1)} %add.479), channel_id=1, source_target_pairs={{0,16},{8,24},{16,0},{24,8},{1,17},{9,25},{17,1},{25,9},{2,18},{10... | collective-permute-start | bytes 49160 | tf_op jit(solution)/shard_map/ppermute | solution.py:24
  267.4 33.3 %copy-start.1 = (s32[128]{0:T(128)S(1)}, s32[128]{0:T(128)}, u32[]{:S(2)}) copy-start(s32[128]{0:T(128)} %param.18) | copy-start | bytes 1540
  (8 other events, 8.0 us)
Sparse Core Ops, SparseCore 0:
  22.6 56.6 all-gather.1
where the time goes:
time: 308 us
  blocking collectives  163 us (53%)
  other arithmetic  64.7 us (21%)
  starting transfers between devices  27.4 us (9%)
  between operations  15.4 us (5%)
  waiting for transfers between devices  15 us (5%)
  local copies, waits for them, and re-layouts  12.4 us (4%)
  matrix products  9.87 us (3%)
    psum x10, blocking collectives, cell_sum(): values = lax.psum(values, axis)  112 us
    all_gather x1, blocking collectives, local(): predicted = lax.all_gather(slab_pred, 'grp', axis=0, tiled=True)  50.4 us
    ppermute x5, waiting for transfers between devices, cell_sum(): lax.ppermute(values, axis, [(i, i ^ step) for i in range(size)])  14.8 us
    another operation x3, other arithmetic, ensemble_weights(): factor = jnp.linalg.cholesky(gram)  12.4 us
    ppermute x3, starting transfers between devices, planes(): low = lax.ppermute(field[:, -1:], CELL, forward)  12.2 us
    another operation x2, other arithmetic, ensemble_weights(): return jax.scipy.linalg.cho_solve((factor, True), cross)  10.5 us
    mul x5, other arithmetic, net(): flow_z = coef_z * diff_z  7.78 us
    dot_general x1, matrix products, local(): jnp.dot(own_columns.T, lax.all_gather(scaled, 'grp', axis=0, tiled=True),...  7.11 us
  transfers between devices with their start and end apart: 14, of which 6 were waited for; matrix products, arithmetic and copies ran while one was open for 24% of the time, Pallas kernels for 0%

commit v1 on v0

--- a/solution.py
+++ b/solution.py
@@ -11,6 +11,12 @@
 compress = 0.5
 inflation = 4.0
 CELL = ("cy", "cz")
+
+
+def tiled_gather(x, axis, dim):
+    size = lax.axis_size(axis)
+    repeats = [size if d == dim else 1 for d in range(x.ndim)]
+    return lax.all_to_all(jnp.tile(x, repeats), axis, split_axis=dim, concat_axis=dim, tiled=True)
 
 
 def cell_sum(values, doubling=False):
@@ -257,7 +263,7 @@
         axis=1,
     )
     slab_pred = cell_sum(picked, doubling=True)
-    predicted = lax.all_gather(slab_pred, "grp", axis=0, tiled=True)
+    predicted = tiled_gather(slab_pred, "grp", 0)
     params = jnp.stack([log_perm, porosity], 1).reshape(local_members, 2 * cells_dev)
     offset = lax.axis_index("grp") * local_members
     own_columns = ensemble_weights(predicted, obs_values, obs_error, noise, offset, local_members)

time: 308 us -> 306 us (level)
  blocking collectives: 163 us -> 112 us
  starting transfers between devices: 27.4 us -> 69.1 us
  waiting for transfers between devices: 15 us -> 20.2 us
    all_gather x1 -> x0, blocking collectives: 50.4 us -> none  [local(): predicted = lax.all_gather(slab_pred, 'grp', axis=0, tiled=True)]
    all_to_all x0 -> x1, starting transfers between devices: none -> 41.8 us  [tiled_gather(): lax.all_to_all(jnp.tile(x, repeats), axis, split_axis=dim, concat_axis=di...]
    all_to_all x0 -> x1, waiting for transfers between devices: none -> 5.23 us  [tiled_gather(): lax.all_to_all(jnp.tile(x, repeats), axis, split_axis=dim, concat_axis=di...]
  transfers between devices with their start and end apart: 14 -> 15, of which waited for: 6 -> 7; matrix products, arithmetic and copies ran while one was open for 24% -> 24% of each run, Pallas kernels for 0% -> 0%
where the time goes in v1:
time: 306 us; the launch traced here: 305 us
  blocking collectives  112 us (37%)
  starting transfers between devices  69.1 us (23%)
  other arithmetic  64.8 us (21%)
  waiting for transfers between devices  20.2 us (7%)
  between operations  15.5 us (5%)
  local copies, waits for them, and re-layouts  13.1 us (4%)
  matrix products  9.87 us (3%)
    psum x10, blocking collectives, cell_sum(): values = lax.psum(values, axis)  112 us
    all_to_all x1, starting transfers between devices, tiled_gather(): lax.all_to_all(jnp.tile(x, repeats), axis, split_axis=dim, concat_axis=di...  41.8 us
    ppermute x5, waiting for transfers between devices, cell_sum(): lax.ppermute(values, axis, [(i, i ^ step) for i in range(size)])  14.8 us
    another operation x3, other arithmetic, ensemble_weights(): factor = jnp.linalg.cholesky(gram)  12.4 us
    ppermute x3, starting transfers between devices, planes(): low = lax.ppermute(field[:, -1:], CELL, forward)  12.2 us
    another operation x2, other arithmetic, ensemble_weights(): return jax.scipy.linalg.cho_solve((factor, True), cross)  10.5 us
    mul x5, other arithmetic, net(): flow_z = coef_z * diff_z  7.76 us
    dot_general x1, matrix products, local(): jnp.dot(own_columns.T, lax.all_gather(scaled, 'grp', axis=0, tiled=True),...  7.11 us
  transfers between devices with their start and end apart: 15, of which 7 were waited for; matrix products, arithmetic and copies ran while one was open for 24% of the time, Pallas kernels for 0%

profile of v1, /device:TPU:1, one launch (start us, length us, event | category | flops | bytes accessed | tf_op | source)
XLA Modules:
  0.0 305.0 jit_solution(15206556631355171594)
XLA Ops:
  7.3 1.2 slice_bitcast_fusion.11
  8.5 1.0 slice_bitcast_fusion.21
  9.5 1.0 slice_bitcast_fusion.17
  10.5 0.8 pad_maximum_fusion.13
  11.3 1.3 collective-permute-start.1
  12.6 0.8 pad_maximum_fusion.12
  13.3 5.0 %collective-permute-start = (f32[16,3,1,16,128]{4,3,0,2,1:T(8,128)}, f32[16,3,1,16,128]{4,3,0,2,1:T(8,128)S(1)}, u32[]{:S(2)}, u32[]{:S(2)}) collective-permute-start(f32[16,3,1,16,128]{4,3,0,2,1:T(8,128)} %pad_maximum_fusion.12), channel_id=1, source_target_pairs={{0,1},{1,2},{2,3},{3,4},{4,5},{5,6},{6,7},{7,8},{8,9},{9,10},{10,1... | collective-permute-start | bytes 1179656 | tf_op jit(solution)/shard_map/ppermute | solution.py:169
  18.3 1.3 pad_maximum_fusion.4
  19.8 1.1 copy-done.23
  20.8 1.7 bitcast_multiply_fusion
  22.6 1.9 gather_fusion
  25.1 0.7 fusion.63
  27.2 1.2 fusion.56
  28.4 1.3 fusion.55
  29.7 1.0 multiply_multiply_fusion.11
  31.0 1.6 fusion.97
  34.2 19.3 %psum.70 = f32[2,16]{1,0:T(2,128)S(1)} all-reduce(f32[2,16]{1,0:T(2,128)S(1)} %pad_maximum_fusion.16), channel_id=1, replica_groups=mesh['grp'=8,'cy'=4,'cz'=8] {'cz'}, use_global_device_ids=true, to_apply=%region_2.3 | all-reduce | flops 32 | bytes 256 | tf_op jit(solution)/shard_map/psum | solution.py:26
  53.5 10.2 %psum.71 = f32[2,16]{1,0:T(2,128)S(1)} all-reduce(f32[2,16]{1,0:T(2,128)S(1)} %psum.70), channel_id=1, replica_groups=mesh['grp'=8,'cy'=4,'cz'=8] {'cy'}, use_global_device_ids=true, to_apply=%region_3.4 | all-reduce | flops 32 | bytes 256 | tf_op jit(solution)/shard_map/psum | solution.py:26
  64.4 1.4 collective-permute-start.2
  65.8 4.0 %collective-permute-start.3 = (f32[16,1,16,128]{3,2,1,0:T(8,128)S(1)}, f32[16,1,16,128]{3,2,1,0:T(8,128)S(1)}, u32[]{:S(2)}, u32[]{:S(2)}) collective-permute-start(f32[16,1,16,128]{3,2,1,0:T(8,128)S(1)} %get-tuple-element.72), channel_id=1, source_target_pairs={{0,1},{1,2},{2,3},{3,4},{4,5},{5,6},{6,7},{7,8},{8,9},{9,10},{10,1... | collective-permute-start | bytes 393224 | tf_op jit(solution)/shard_map/ppermute | solution.py:186
  69.8 2.0 multiply_multiply_fusion.10
  71.8 1.2 broadcast_divide_fusion
  73.5 1.1 multiply_subtract_fusion.8
  76.6 14.2 %psum.72 = f32[3,16]{1,0:T(4,128)S(1)} all-reduce(f32[3,16]{1,0:T(4,128)S(1)} %pad_maximum_fusion.14), channel_id=1, replica_groups=mesh['grp'=8,'cy'=4,'cz'=8] {'cz'}, use_global_device_ids=true, to_apply=%region_7.8 | all-reduce | flops 48 | bytes 384 | tf_op jit(solution)/shard_map/psum | solution.py:26
  90.9 6.0 %psum.73 = f32[3,16]{1,0:T(4,128)S(1)} all-reduce(f32[3,16]{1,0:T(4,128)S(1)} %psum.72), channel_id=1, replica_groups=mesh['grp'=8,'cy'=4,'cz'=8] {'cy'}, use_global_device_ids=true, to_apply=%region_8.9 | all-reduce | flops 48 | bytes 384 | tf_op jit(solution)/shard_map/psum | solution.py:26
  97.5 2.6 multiply_subtract_fusion.1
  100.4 1.3 collective-permute-start.4
  101.7 4.2 %collective-permute-start.5 = (f32[16,1,16,128]{3,2,1,0:T(8,128)S(1)}, f32[16,1,16,128]{3,2,1,0:T(8,128)S(1)}, u32[]{:S(2)}, u32[]{:S(2)}) collective-permute-start(f32[16,1,16,128]{3,2,1,0:T(8,128)S(1)} %get-tuple-element.70), channel_id=1, source_target_pairs={{0,1},{1,2},{2,3},{3,4},{4,5},{5,6},{6,7},{7,8},{8,9},{9,10},{10,1... | collective-permute-start | bytes 393224 | tf_op jit(solution)/shard_map/ppermute | solution.py:186
  105.9 2.0 multiply_multiply_fusion.9
  108.4 1.3 multiply_subtract_fusion.6
  111.4 0.7 multiply_reduce_fusion.10
  112.2 14.7 %psum.74 = f32[4,16]{1,0:T(4,128)} all-reduce(f32[4,16]{1,0:T(4,128)S(1)} %pad_maximum_fusion.15), channel_id=1, replica_groups=mesh['grp'=8,'cy'=4,'cz'=8] {'cz'}, use_global_device_ids=true, to_apply=%region_13.14 | all-reduce | flops 64 | bytes 512 | tf_op jit(solution)/shard_map/psum | solution.py:26
  127.0 7.5 %psum.75 = f32[4,16]{1,0:T(4,128)} all-reduce(f32[4,16]{1,0:T(4,128)} %psum.74), channel_id=1, replica_groups=mesh['grp'=8,'cy'=4,'cz'=8] {'cy'}, use_global_device_ids=true, to_apply=%region_14.15 | all-reduce | flops 64 | bytes 512 | tf_op jit(solution)/shard_map/psum | solution.py:26
  134.5 0.8 sqrt_bitcast_fusion.1
  135.3 0.8 bitcast_divide_fusion.4
  136.2 2.4 copy_subtract_fusion
  139.0 1.4 collective-permute-start.6
  140.4 4.0 %collective-permute-start.7 = (f32[16,1,16,128]{3,2,1,0:T(8,128)S(1)}, f32[16,1,16,128]{3,2,1,0:T(8,128)S(1)}, u32[]{:S(2)}, u32[]{:S(2)}) collective-permute-start(f32[16,1,16,128]{3,2,1,0:T(8,128)S(1)} %get-tuple-element.68), channel_id=1, source_target_pairs={{0,1},{1,2},{2,3},{3,4},{4,5},{5,6},{6,7},{7,8},{8,9},{9,10},{10,1... | collective-permute-start | bytes 393224 | tf_op jit(solution)/shard_map/ppermute | solution.py:186
  144.5 1.2 multiply_multiply_fusion.8
  146.4 1.2 multiply_subtract_fusion.4
  148.8 0.9 multiply_reduce_fusion.2
  149.7 14.1 %psum.76 = f32[5,16]{1,0:T(8,128)S(1)} all-reduce(f32[5,16]{1,0:T(8,128)S(1)} %stack.169), channel_id=1, replica_groups=mesh['grp'=8,'cy'=4,'cz'=8] {'cz'}, use_global_device_ids=true, to_apply=%region_20.21 | all-reduce | flops 80 | bytes 640 | tf_op jit(solution)/shard_map/psum | solution.py:26
  163.8 7.9 %psum.77 = f32[5,16]{1,0:T(8,128)S(1)} all-reduce(f32[5,16]{1,0:T(8,128)S(1)} %psum.76), channel_id=1, replica_groups=mesh['grp'=8,'cy'=4,'cz'=8] {'cy'}, use_global_device_ids=true, to_apply=%region_21.22 | all-reduce | flops 80 | bytes 640 | tf_op jit(solution)/shard_map/psum | solution.py:26
  171.8 2.3 multiply_reduce_fusion.1
  174.1 12.3 %psum.78 = f32[16]{0:T(128)S(1)} all-reduce(f32[16]{0:T(128)S(1)} %multiply_reduce_fusion.1), channel_id=1, replica_groups=mesh['grp'=8,'cy'=4,'cz'=8] {'cz'}, use_global_device_ids=true, to_apply=%region_23.24 | all-reduce | flops 16 | bytes 128 | tf_op jit(solution)/shard_map/psum | solution.py:26
  186.4 6.1 %psum.79 = f32[16]{0:T(128)S(1)} all-reduce(f32[16]{0:T(128)S(1)} %psum.78), channel_id=1, replica_groups=mesh['grp'=8,'cy'=4,'cz'=8] {'cy'}, use_global_device_ids=true, to_apply=%region_24.25 | all-reduce | flops 16 | bytes 128 | tf_op jit(solution)/shard_map/psum | solution.py:26
  192.6 2.1 multiply_add_fusion
  194.7 1.6 fusion.19
  196.6 1.0 multiply_reduce_fusion
  197.8 2.5 collective-permute-done.8
  200.3 3.5 %collective-permute-done.9 = f32[16,256]{1,0:T(8,128)S(1)} collective-permute-done((f32[16,256]{1,0:T(8,128)S(1)}, f32[16,256]{1,0:T(8,128)S(1)}, u32[]{:S(2)}, u32[]{:S(2)}) %collective-permute-start.9) | collective-permute-done | bytes 16416 | tf_op jit(solution)/shard_map/ppermute | solution.py:30
  203.8 2.3 collective-permute-start.10
  206.1 4.4 %collective-permute-done.10 = f32[16,256]{1,0:T(8,128)S(1)} collective-permute-done((f32[16,256]{1,0:T(8,128)S(1)}, f32[16,256]{1,0:T(8,128)S(1)}, u32[]{:S(2)}, u32[]{:S(2)}) %collective-permute-start.10) | collective-permute-done | bytes 16416 | tf_op jit(solution)/shard_map/ppermute | solution.py:30
  210.5 1.4 collective-permute-start.11
  211.8 1.2 collective-permute-done.11
  213.1 0.9 collective-permute-start.12
  214.0 3.2 %collective-permute-done.12 = f32[16,256]{1,0:T(8,128)S(1)} collective-permute-done((f32[16,256]{1,0:T(8,128)S(1)}, f32[16,256]{1,0:T(8,128)S(1)}, u32[]{:S(2)}, u32[]{:S(2)}) %collective-permute-start.12) | collective-permute-done | bytes 16416 | tf_op jit(solution)/shard_map/ppermute | solution.py:30
  217.8 41.8 %all-to-all-start = ((f32[8,16,256]{2,1,0:T(8,128)}), f32[8,16,256]{2,1,0:T(8,128)S(1)}, u32[]{:S(2)}, u32[]{:S(2)}) async-start(f32[8,16,256]{2,1,0:T(8,128)} %tile.2), calls=%async_computation | async-start | bytes 262144 | tf_op jit(solution)/shard_map/all_to_all | solution.py:19
  259.6 5.2 %all-to-all-done = f32[8,16,256]{2,1,0:T(8,128)S(1)} async-done(((f32[8,16,256]{2,1,0:T(8,128)}), f32[8,16,256]{2,1,0:T(8,128)S(1)}, u32[]{:S(2)}, u32[]{:S(2)}) %all-to-all-start) | async-done | bytes 131104 | tf_op jit(solution)/shard_map/all_to_all | solution.py:19
  265.3 11.7 %cholesky.17 = f32[128,128]{1,0:T(8,128)S(1)} custom-call(f32[128,128]{1,0:T(8,128)S(1)} %fusion.74), custom_call_target="Cholesky" | custom-call | tf_op jit(solution)/shard_map/jit(cholesky)/cholesky | solution.py:144
  278.4 9.8 %custom-call.10 = f32[1,128,128]{1,2,0:T(8,128)S(1)} custom-call(f32[1,128,128]{2,1,0:T(8,128)S(1)} %fusion.68), custom_call_target="InvertDiagBlocksLowerTriangular" | custom-call | tf_op jit(solution)/shard_map/jit(_cho_solve)/triangular_solve | solution.py:145
  288.2 1.0 fusion.57
  289.7 7.1 %fusion = f32[2,8,128,128]{3,1,2,0:T(8,128)S(1)} fusion(f32[128,16]{1,0:T(8,128)S(1)} %fusion.69, f32[128,16384]{1,0:T(8,128)} %all-gather.2.cloned.1.call-done, f32[2,8,128,128]{3,2,1,0:T(8,128)S(1)} %bitcast.508), kind=kOutput, calls=%fused_computation.3 | convolution fusion | flops 402915328 | bytes 10493952 | tf_op jit(solution)/shard_map/dot_general | solution.py:272
  297.1 1.1 slice_bitcast_fusion
  (228 shorter events, 16.0 us)
Async XLA Ops:
  7.2 15.4 %copy-start = (s32[128]{0:T(128)S(1)}, s32[128]{0:T(128)}, u32[]{:S(2)}) copy-start(s32[128]{0:T(128)} %param.18) | copy-start | bytes 1540
  7.2 19.2 %copy-start.2 = (f32[16,2,4,16,128]{4,3,2,1,0:T(8,128)S(1)}, f32[16,2,4,16,128]{4,3,2,1,0:T(8,128)}, u32[]{:S(2)}) copy-start(f32[16,2,4,16,128]{4,3,2,1,0:T(8,128)} %param.10) | copy-start | bytes 3145732
  7.2 18.9 %copy-start.3 = (f32[16,4,16,128]{3,2,1,0:T(8,128)S(1)}, f32[16,4,16,128]{3,2,1,0:T(8,128)}, u32[]{:S(2)}) copy-start(f32[16,4,16,128]{3,2,1,0:T(8,128)} %param.13) | copy-start | bytes 1572868
  7.2 15.3 %copy-start.53 = (s32[256]{0:T(256)S(1)}, s32[256]{0:T(256)}, u32[]{:S(2)}) copy-start(s32[256]{0:T(256)} %param.19) | copy-start | bytes 3076
  7.2 282.5 %all-gather.2.cloned.1.call-start = ((), (), s32[]{:S(2)}) async-start(), calls=%async_computation.1 | async-start | bytes 9437184 | tf_op jit(solution)/shard_map/all_gather | solution.py:274
  10.5 16.2 %copy-start.27 = (f32[16,4,16,128]{3,2,1,0:T(8,128)S(1)}, f32[16,4,16,128]{3,2,1,0:T(8,128)}, u32[]{:S(2)}) copy-start(f32[16,4,16,128]{3,2,1,0:T(8,128)} %param.11) | copy-start | bytes 1572868
  11.3 15.3 %collective-permute-start.1 = (f32[16,3,1,16,128]{4,3,0,2,1:T(8,128)}, f32[16,3,1,16,128]{4,3,0,2,1:T(8,128)S(1)}, u32[]{:S(2)}, u32[]{:S(2)}) collective-permute-start(f32[16,3,1,16,128]{4,3,0,2,1:T(8,128)} %pad_maximum_fusion.13), channel_id=1, source_target_pairs={{1,0},{2,1},{3,2},{4,3},{5,4},{6,5},{7,6},{8,7},{9,8},{10,9},{11,1... | collective-permute-start | bytes 1179656 | tf_op jit(solution)/shard_map/ppermute | solution.py:170
  13.3 13.3 %collective-permute-start = (f32[16,3,1,16,128]{4,3,0,2,1:T(8,128)}, f32[16,3,1,16,128]{4,3,0,2,1:T(8,128)S(1)}, u32[]{:S(2)}, u32[]{:S(2)}) collective-permute-start(f32[16,3,1,16,128]{4,3,0,2,1:T(8,128)} %pad_maximum_fusion.12), channel_id=1, source_target_pairs={{0,1},{1,2},{2,3},{3,4},{4,5},{5,6},{6,7},{7,8},{8,9},{9,10},{10,1... | collective-permute-start | bytes 1179656 | tf_op jit(solution)/shard_map/ppermute | solution.py:169
  25.8 80.1 %copy-start.43 = (f32[128]{0:T(128)}, f32[128]{0:T(128)S(1)}, u32[]{:S(2)}) copy-start(f32[128]{0:T(128)S(1)} %compare_convert_fusion) | copy-start | bytes 1540
  25.8 80.1 %copy-start.44 = (f32[16]{0:T(128)}, f32[16]{0:T(128)S(1)}, u32[]{:S(2)}) copy-start(f32[16]{0:T(128)S(1)} %compare_convert_fusion.1) | copy-start | bytes 196
  26.6 4.1 %copy-start.37 = (f32[16,3,1,16,128]{4,3,0,2,1:T(8,128)}, f32[16,3,1,16,128]{4,3,0,2,1:T(8,128)S(1)}, u32[]{:S(2)}) copy-start(f32[16,3,1,16,128]{4,3,0,2,1:T(8,128)S(1)} %collective-permute-done.1) | copy-start | bytes 1179652
  26.6 4.1 %copy-start.38 = (f32[16,3,1,16,128]{4,3,0,2,1:T(8,128)}, f32[16,3,1,16,128]{4,3,0,2,1:T(8,128)S(1)}, u32[]{:S(2)}) copy-start(f32[16,3,1,16,128]{4,3,0,2,1:T(8,128)S(1)} %collective-permute-done) | copy-start | bytes 1179652
  29.7 3.1 %copy-start.8 = (f32[16,4,16,128]{3,2,1,0:T(8,128)S(1)}, f32[16,4,16,128]{3,2,1,0:T(8,128)}, u32[]{:S(2)}) copy-start(f32[16,4,16,128]{3,2,1,0:T(8,128)} %param.12) | copy-start | bytes 1572868
  30.8 3.2 %copy-start.13 = (f32[16,4,16,128]{3,2,1,0:T(8,128)}, f32[16,4,16,128]{3,2,1,0:T(8,128)S(1)}, u32[]{:S(2)}) copy-start(f32[16,4,16,128]{3,2,1,0:T(8,128)S(1)} %get-tuple-element.24) | copy-start | bytes 1572868
  30.8 3.2 %copy-start.15 = (f32[16,4,16,128]{3,2,1,0:T(8,128)}, f32[16,4,16,128]{3,2,1,0:T(8,128)S(1)}, u32[]{:S(2)}) copy-start(f32[16,4,16,128]{3,2,1,0:T(8,128)S(1)} %get-tuple-element.36) | copy-start | bytes 1572868
  33.9 41.9 %copy-start.5 = (f32[16,1,4,16,128]{4,3,2,0,1:T(8,128)}, f32[16,1,4,16,128]{4,3,2,0,1:T(8,128)S(1)}, u32[]{:S(2)}) copy-start(f32[16,1,4,16,128]{4,3,2,0,1:T(8,128)S(1)} %fusion.45) | copy-start | bytes 1572868
  63.7 33.1 %copy-start.47 = (f32[2,16]{1,0:T(2,128)}, f32[2,16]{1,0:T(2,128)S(1)}, u32[]{:S(2)}) copy-start(f32[2,16]{1,0:T(2,128)S(1)} %psum.71) | copy-start | bytes 388
  63.8 10.8 %copy-start.17 = (f32[16,5,16,128]{3,2,1,0:T(8,128)S(1)}, f32[16,5,16,128]{3,2,1,0:T(8,128)}, u32[]{:S(2)}) copy-start(f32[16,5,16,128]{3,2,1,0:T(8,128)} %get-tuple-element.28) | copy-start | bytes 1966084
  63.8 10.8 %copy-start.20 = (f32[16,5,16,128]{3,2,1,0:T(8,128)S(1)}, f32[16,5,16,128]{3,2,1,0:T(8,128)}, u32[]{:S(2)}) copy-start(f32[16,5,16,128]{3,2,1,0:T(8,128)} %get-tuple-element.34) | copy-start | bytes 1966084
  64.0 11.3 %copy-start.12 = (f32[16,2,4,16,128]{4,3,2,0,1:T(8,128)}, f32[16,2,4,16,128]{4,3,2,0,1:T(8,128)S(1)}, u32[]{:S(2)}) copy-start(f32[16,2,4,16,128]{4,3,2,0,1:T(8,128)S(1)} %multiply_subtract_fusion.2) | copy-start | bytes 3145732
  64.4 9.1 %collective-permute-start.2 = (f32[16,1,16,128]{3,2,1,0:T(8,128)S(1)}, f32[16,1,16,128]{3,2,1,0:T(8,128)S(1)}, u32[]{:S(2)}, u32[]{:S(2)}) collective-permute-start(f32[16,1,16,128]{3,2,1,0:T(8,128)S(1)} %get-tuple-element.71), channel_id=1, source_target_pairs={{1,0},{2,1},{3,2},{4,3},{5,4},{6,5},{7,6},{8,7},{9,8},{10,9},{11,1... | collective-permute-start | bytes 393224 | tf_op jit(solution)/shard_map/ppermute | solution.py:187
  65.8 7.7 %collective-permute-start.3 = (f32[16,1,16,128]{3,2,1,0:T(8,128)S(1)}, f32[16,1,16,128]{3,2,1,0:T(8,128)S(1)}, u32[]{:S(2)}, u32[]{:S(2)}) collective-permute-start(f32[16,1,16,128]{3,2,1,0:T(8,128)S(1)} %get-tuple-element.72), channel_id=1, source_target_pairs={{0,1},{1,2},{2,3},{3,4},{4,5},{5,6},{6,7},{7,8},{8,9},{9,10},{10,1... | collective-permute-start | bytes 393224 | tf_op jit(solution)/shard_map/ppermute | solution.py:186
  96.9 11.5 %copy-start.45 = (f32[3,16]{1,0:T(4,128)}, f32[3,16]{1,0:T(4,128)S(1)}, u32[]{:S(2)}) copy-start(f32[3,16]{1,0:T(4,128)S(1)} %psum.73) | copy-start | bytes 580
  96.9 3.5 %copy-start.29 = (f32[16,4,16,128]{3,2,1,0:T(8,128)S(1)}, f32[16,4,16,128]{3,2,1,0:T(8,128)}, u32[]{:S(2)}) copy-start(f32[16,4,16,128]{3,2,1,0:T(8,128)} %copy-done.28) | copy-start | bytes 1572868
  97.5 11.0 %copy-start.51 = (f32[16]{0:T(128)}, f32[16]{0:T(128)S(1)}, u32[]{:S(2)}) copy-start(f32[16]{0:T(128)S(1)} %get-tuple-element.98) | copy-start | bytes 196
  97.5 12.3 %copy-start.18 = (f32[16,5,16,128]{3,2,1,0:T(8,128)S(1)}, f32[16,5,16,128]{3,2,1,0:T(8,128)}, u32[]{:S(2)}) copy-start(f32[16,5,16,128]{3,2,1,0:T(8,128)} %get-tuple-element.28) | copy-start | bytes 1966084
  97.5 12.3 %copy-start.21 = (f32[16,5,16,128]{3,2,1,0:T(8,128)S(1)}, f32[16,5,16,128]{3,2,1,0:T(8,128)}, u32[]{:S(2)}) copy-start(f32[16,5,16,128]{3,2,1,0:T(8,128)} %get-tuple-element.34) | copy-start | bytes 1966084
  100.1 10.3 %copy-start.9 = (f32[16,4,16,128]{3,2,1,0:T(8,128)S(1)}, f32[16,4,16,128]{3,2,1,0:T(8,128)}, u32[]{:S(2)}) copy-start(f32[16,4,16,128]{3,2,1,0:T(8,128)} %param.12) | copy-start | bytes 1572868
  100.4 8.0 %collective-permute-start.4 = (f32[16,1,16,128]{3,2,1,0:T(8,128)S(1)}, f32[16,1,16,128]{3,2,1,0:T(8,128)S(1)}, u32[]{:S(2)}, u32[]{:S(2)}) collective-permute-start(f32[16,1,16,128]{3,2,1,0:T(8,128)S(1)} %get-tuple-element.69), channel_id=1, source_target_pairs={{1,0},{2,1},{3,2},{4,3},{5,4},{6,5},{7,6},{8,7},{9,8},{10,9},{11,1... | collective-permute-start | bytes 393224 | tf_op jit(solution)/shard_map/ppermute | solution.py:187
  101.7 6.7 %collective-permute-start.5 = (f32[16,1,16,128]{3,2,1,0:T(8,128)S(1)}, f32[16,1,16,128]{3,2,1,0:T(8,128)S(1)}, u32[]{:S(2)}, u32[]{:S(2)}) collective-permute-start(f32[16,1,16,128]{3,2,1,0:T(8,128)S(1)} %get-tuple-element.70), channel_id=1, source_target_pairs={{0,1},{1,2},{2,3},{3,4},{4,5},{5,6},{6,7},{7,8},{8,9},{9,10},{10,1... | collective-permute-start | bytes 393224 | tf_op jit(solution)/shard_map/ppermute | solution.py:186
  108.1 3.3 %copy-start.6 = (f32[16,1,4,16,128]{4,3,2,0,1:T(8,128)S(1)}, f32[16,1,4,16,128]{4,3,2,0,1:T(8,128)}, u32[]{:S(2)}) copy-start(f32[16,1,4,16,128]{4,3,2,0,1:T(8,128)} %copy-done.5) | copy-start | bytes 1572868
  108.1 3.3 %copy-start.11 = (f32[16,2,4,16,128]{4,3,2,1,0:T(8,128)S(1)}, f32[16,2,4,16,128]{4,3,2,1,0:T(8,128)}, u32[]{:S(2)}) copy-start(f32[16,2,4,16,128]{4,3,2,1,0:T(8,128)} %broadcast_divide_fusion) | copy-start | bytes 3145732
  134.4 4.5 %copy-start.31 = (f32[16,4,16,128]{3,2,1,0:T(8,128)S(1)}, f32[16,4,16,128]{3,2,1,0:T(8,128)}, u32[]{:S(2)}) copy-start(f32[16,4,16,128]{3,2,1,0:T(8,128)} %copy-done.30) | copy-start | bytes 1572868
  134.4 10.0 %copy-start.14 = (f32[16,4,16,128]{3,2,1,0:T(8,128)S(1)}, f32[16,4,16,128]{3,2,1,0:T(8,128)}, u32[]{:S(2)}) copy-start(f32[16,4,16,128]{3,2,1,0:T(8,128)} %copy-done.13) | copy-start | bytes 1572868
  134.4 10.0 %copy-start.16 = (f32[16,4,16,128]{3,2,1,0:T(8,128)S(1)}, f32[16,4,16,128]{3,2,1,0:T(8,128)}, u32[]{:S(2)}) copy-start(f32[16,4,16,128]{3,2,1,0:T(8,128)} %copy-done.15) | copy-start | bytes 1572868
  134.5 10.0 %copy-start.25 = (f32[16,4,16,128]{3,2,1,0:T(8,128)S(1)}, f32[16,4,16,128]{3,2,1,0:T(8,128)}, u32[]{:S(2)}) copy-start(f32[16,4,16,128]{3,2,1,0:T(8,128)} %get-tuple-element.30) | copy-start | bytes 1572868
  134.5 10.0 %copy-start.26 = (f32[16,4,16,128]{3,2,1,0:T(8,128)S(1)}, f32[16,4,16,128]{3,2,1,0:T(8,128)}, u32[]{:S(2)}) copy-start(f32[16,4,16,128]{3,2,1,0:T(8,128)} %get-tuple-element.50) | copy-start | bytes 1572868
  136.1 10.2 %copy-start.49 = (f32[16]{0:T(128)}, f32[16]{0:T(128)S(1)}, u32[]{:S(2)}) copy-start(f32[16]{0:T(128)S(1)} %get-tuple-element.91) | copy-start | bytes 196
  136.1 10.2 %copy-start.40 = (f32[16,1,16,128]{3,2,1,0:T(8,128)S(1)}, f32[16,1,16,128]{3,2,1,0:T(8,128)}, u32[]{:S(2)}) copy-start(f32[16,1,16,128]{3,2,1,0:T(8,128)} %copy-done.39) | copy-start | bytes 393220
  136.1 11.4 %copy-start.19 = (f32[16,5,16,128]{3,2,1,0:T(8,128)S(1)}, f32[16,5,16,128]{3,2,1,0:T(8,128)}, u32[]{:S(2)}) copy-start(f32[16,5,16,128]{3,2,1,0:T(8,128)} %get-tuple-element.28) | copy-start | bytes 1966084
  136.2 11.4 %copy-start.22 = (f32[16,5,16,128]{3,2,1,0:T(8,128)S(1)}, f32[16,5,16,128]{3,2,1,0:T(8,128)}, u32[]{:S(2)}) copy-start(f32[16,5,16,128]{3,2,1,0:T(8,128)} %get-tuple-element.34) | copy-start | bytes 1966084
  138.6 10.2 %copy-start.4 = (f32[16,2,4,16,128]{4,3,2,1,0:T(8,128)}, f32[16,2,4,16,128]{4,3,2,1,0:T(8,128)S(1)}, u32[]{:S(2)}) copy-start(f32[16,2,4,16,128]{4,3,2,1,0:T(8,128)S(1)} %copy_subtract_fusion) | copy-start | bytes 3145732
  138.6 9.1 %copy-start.10 = (f32[16,4,16,128]{3,2,1,0:T(8,128)S(1)}, f32[16,4,16,128]{3,2,1,0:T(8,128)}, u32[]{:S(2)}) copy-start(f32[16,4,16,128]{3,2,1,0:T(8,128)} %param.12) | copy-start | bytes 1572868
  139.0 7.2 %collective-permute-start.6 = (f32[16,1,16,128]{3,2,1,0:T(8,128)S(1)}, f32[16,1,16,128]{3,2,1,0:T(8,128)S(1)}, u32[]{:S(2)}, u32[]{:S(2)}) collective-permute-start(f32[16,1,16,128]{3,2,1,0:T(8,128)S(1)} %get-tuple-element.67), channel_id=1, source_target_pairs={{1,0},{2,1},{3,2},{4,3},{5,4},{6,5},{7,6},{8,7},{9,8},{10,9},{11,1... | collective-permute-start | bytes 393224 | tf_op jit(solution)/shard_map/ppermute | solution.py:187
  140.4 5.9 %collective-permute-start.7 = (f32[16,1,16,128]{3,2,1,0:T(8,128)S(1)}, f32[16,1,16,128]{3,2,1,0:T(8,128)S(1)}, u32[]{:S(2)}, u32[]{:S(2)}) collective-permute-start(f32[16,1,16,128]{3,2,1,0:T(8,128)S(1)} %get-tuple-element.68), channel_id=1, source_target_pairs={{0,1},{1,2},{2,3},{3,4},{4,5},{5,6},{6,7},{7,8},{8,9},{9,10},{10,1... | collective-permute-start | bytes 393224 | tf_op jit(solution)/shard_map/ppermute | solution.py:186
  145.9 2.9 copy-start.7
  148.3 44.2 %copy-start.42 = (f32[4,16]{1,0:T(4,128)S(1)}, f32[4,16]{1,0:T(4,128)}, u32[]{:S(2)}) copy-start(f32[4,16]{1,0:T(4,128)} %psum.75) | copy-start | bytes 772
  148.3 44.2 %copy-start.46 = (f32[3,16]{1,0:T(4,128)S(1)}, f32[3,16]{1,0:T(4,128)}, u32[]{:S(2)}) copy-start(f32[3,16]{1,0:T(4,128)} %copy-done.45) | copy-start | bytes 580
  148.3 44.2 %copy-start.48 = (f32[2,16]{1,0:T(2,128)S(1)}, f32[2,16]{1,0:T(2,128)}, u32[]{:S(2)}) copy-start(f32[2,16]{1,0:T(2,128)} %copy-done.47) | copy-start | bytes 388
  148.3 44.2 %copy-start.50 = (f32[16]{0:T(128)S(1)}, f32[16]{0:T(128)}, u32[]{:S(2)}) copy-start(f32[16]{0:T(128)} %copy-done.49) | copy-start | bytes 196
  148.3 44.2 %copy-start.52 = (f32[16]{0:T(128)S(1)}, f32[16]{0:T(128)}, u32[]{:S(2)}) copy-start(f32[16]{0:T(128)} %copy-done.51) | copy-start | bytes 196
  148.3 44.2 %copy-start.55 = (f32[16]{0:T(128)S(1)}, f32[16]{0:T(128)}, u32[]{:S(2)}) copy-start(f32[16]{0:T(128)} %get-tuple-element.97) | copy-start | bytes 196
  174.0 22.5 %copy-start.41 = (f32[128,256]{1,0:T(8,128)S(1)}, f32[128,256]{1,0:T(8,128)}, u32[]{:S(2)}) copy-start(f32[128,256]{1,0:T(8,128)} %fusion.63) | copy-start | bytes 393220
  174.1 22.5 %copy-start.54 = (s32[256]{0:T(256)S(1)}, s32[256]{0:T(256)}, u32[]{:S(2)}) copy-start(s32[256]{0:T(256)} %get-tuple-element.15) | copy-start | bytes 3076
  174.1 85.5 %copy-start.56 = (f32[256]{0:T(256)S(1)}, f32[256]{0:T(256)}, u32[]{:S(2)}) copy-start(f32[256]{0:T(256)} %param.16) | copy-start | bytes 3076
  192.6 95.6 %copy-start.57 = (f32[256]{0:T(256)S(1)}, f32[256]{0:T(256)}, u32[]{:S(2)}) copy-start(f32[256]{0:T(256)} %param.15) | copy-start | bytes 3076
  194.7 95.0 %copy-start.24 = (f32[16,2,4,16,128]{4,3,2,1,0:T(8,128)S(1)}, f32[16,2,4,16,128]{4,3,2,1,0:T(8,128)}, u32[]{:S(2)}) copy-start(f32[16,2,4,16,128]{4,3,2,1,0:T(8,128)} %copy-done.23) | copy-start | bytes 3145732
  197.6 2.7 collective-permute-start.8
  200.3 3.5 %collective-permute-start.9 = (f32[16,256]{1,0:T(8,128)S(1)}, f32[16,256]{1,0:T(8,128)S(1)}, u32[]{:S(2)}, u32[]{:S(2)}) collective-permute-start(f32[16,256]{1,0:T(8,128)S(1)} %add.476), channel_id=1, source_target_pairs={{0,2},{1,3},{2,0},{3,1},{4,6},{5,7},{6,4},{7,5},{8,10},{9,11},{10,... | collective-permute-start | bytes 49160 | tf_op jit(solution)/shard_map/ppermute | solution.py:30
  203.8 6.7 %collective-permute-start.10 = (f32[16,256]{1,0:T(8,128)S(1)}, f32[16,256]{1,0:T(8,128)S(1)}, u32[]{:S(2)}, u32[]{:S(2)}) collective-permute-start(f32[16,256]{1,0:T(8,128)S(1)} %add.477), channel_id=1, source_target_pairs={{0,4},{1,5},{2,6},{3,7},{4,0},{5,1},{6,2},{7,3},{8,12},{9,13},{10,... | collective-permute-start | bytes 49160 | tf_op jit(solution)/shard_map/ppermute | solution.py:30
  210.5 2.6 collective-permute-start.11
  213.1 4.1 %collective-permute-start.12 = (f32[16,256]{1,0:T(8,128)S(1)}, f32[16,256]{1,0:T(8,128)S(1)}, u32[]{:S(2)}, u32[]{:S(2)}) collective-permute-start(f32[16,256]{1,0:T(8,128)S(1)} %add.479), channel_id=1, source_target_pairs={{0,16},{8,24},{16,0},{24,8},{1,17},{9,25},{17,1},{25,9},{2,18},{10... | collective-permute-start | bytes 49160 | tf_op jit(solution)/shard_map/ppermute | solution.py:30
  217.8 47.0 %all-to-all-start = ((f32[8,16,256]{2,1,0:T(8,128)}), f32[8,16,256]{2,1,0:T(8,128)S(1)}, u32[]{:S(2)}, u32[]{:S(2)}) async-start(f32[8,16,256]{2,1,0:T(8,128)} %tile.2), calls=%async_computation | async-start | bytes 262144 | tf_op jit(solution)/shard_map/all_to_all | solution.py:19
  264.9 33.3 %copy-start.1 = (s32[128]{0:T(128)S(1)}, s32[128]{0:T(128)}, u32[]{:S(2)}) copy-start(s32[128]{0:T(128)} %param.18) | copy-start | bytes 1540
  (9 other events, 9.6 us)
Sparse Core Ops, SparseCore 0:
  22.6 56.6 all-gather.1
